TPU v7x, 32 devices: a whole 2x2x4 slice. The times are simulated.
32 devices in a mesh: groups: 2 (over x), dp: 16 (over z, y, core).
Axes of the slice: x: 2, y: 2, z: 4, core: 2. Of those that a mesh axis runs over, the one named last changes fastest.
Arguments:
- layer_input: bfloat16 [8192, 8192], P(('groups', 'dp')), parts along dimension 0, may hold values from -6 to 6
- grad_values: bfloat16 [8192, 1024], P(('groups', 'dp')), parts along dimension 0, may hold values from -6 to 6
- base_weight: bfloat16 [8192, 1024], P('dp'), may hold values from -0.0625 to 0.0625
- tile_ids: int32 [32], P(('groups', 'dp')), parts along dimension 0, may hold values from 0 to 511, as said below
- tile_delta: bfloat16 [32, 128, 128], P(('groups', 'dp')), parts along dimension 0, may hold values from -0.1875 to 0.1875
Outputs:
- grad_input: bfloat16 [8192, 8192], P(('groups', 'dp')), parts along dimension 0
- grad_tiles: float32 [32, 128, 128], P(('groups', 'dp')), parts along dimension 0
There are 2 independent parts, one for each index of `groups`. A program takes and returns all parts, laid end to end along the dimension named above; an argument that names none is the same for every part. Nothing has to cross between parts.
Inputs may be any that keep to these rules, and one draw needn't show every extreme that they name: `tile_ids`: the 16 tile numbers are distinct; every tile of some tile row is listed.
All inputs are finite; a program needn't handle non-finite values.
Results may differ from a plain program's by a relative error of at most 0.0034.
Values may be sent and summed in bfloat16 or wider, within the bound.
No kernel may reach another device: no remote copies, remote signals or barrier semaphores. Data moves between devices by JAX's collectives and lax.ppermute only.
A program may use at most 128 MiB of HBM per device.

v0:
```python
import math
import jax
import jax.numpy as jnp
from jax import lax
from jax.sharding import PartitionSpec as P

TILE = 128
ROW_TILES = 64
COL_TILES = 8


def delta_matrix(tile_ids, tile_delta):
    tile_rows = tile_ids // COL_TILES
    tile_cols = tile_ids % COL_TILES
    field = jnp.zeros((ROW_TILES, TILE, COL_TILES, TILE), tile_delta.dtype)
    field = field.at[tile_rows, :, tile_cols, :].set(tile_delta)
    return field.reshape(ROW_TILES * TILE, COL_TILES * TILE)


def whole_field(all_ids, tile_delta):
    all_deltas = lax.all_gather(tile_delta, "dp", axis=0, tiled=True)
    return delta_matrix(all_ids, all_deltas)


def body(layer_input, grad_values, base_weight, tile_ids, tile_delta):
    all_ids = lax.all_gather(tile_ids, "dp", axis=0, tiled=True)
    own_rows = base_weight.shape[0]
    field = whole_field(all_ids, tile_delta)
    first_row = lax.axis_index("dp") * own_rows
    own_field = lax.dynamic_slice_in_dim(field, first_row, own_rows, 0)
    merged = (base_weight.astype(jnp.float32) + own_field.astype(jnp.float32)).astype(jnp.bfloat16)
    grad_input = lax.dot_general(
        grad_values,
        lax.all_gather(merged, "dp", axis=0, tiled=True),
        (((1,), (1,)), ((), ())),
        preferred_element_type=jnp.float32,
    ).astype(jnp.bfloat16)
    tokens_here = layer_input.shape[0]
    input_panels = layer_input.reshape(tokens_here, ROW_TILES, TILE)
    grad_panels = grad_values.reshape(tokens_here, COL_TILES, TILE)
    rows_taken = jnp.take(input_panels, all_ids // COL_TILES, axis=1)
    cols_taken = jnp.take(grad_panels, all_ids % COL_TILES, axis=1)
    summed = lax.psum_scatter(
        jnp.einsum("tja,tjb->jab", rows_taken, cols_taken, preferred_element_type=jnp.float32),
        "dp",
        scatter_dimension=0,
        tiled=True,
    )
    factor = 1.0 / math.sqrt(tokens_here * lax.axis_size("dp"))
    return (grad_input, summed * factor)


def solution(mesh):
    placed = (
        P(("groups", "dp"), None),
        P(("groups", "dp"), None),
        P("dp", None),
        P(("groups", "dp")),
        P(("groups", "dp"), None, None),
    )
    return jax.shard_map(
        body,
        mesh=mesh,
        in_specs=placed,
        out_specs=(P(("groups", "dp"), None), P(("groups", "dp"), None, None)),
        check_vma=False,
    )
```

profile of v0, /device:TPU:0, one launch (start us, length us, event | category | flops | bytes accessed | tf_op | source)
XLA Modules:
  0.0 252.2 jit_solution(3247052467888750626)
XLA Ops:
  7.2 0.0 copy-start.2
  7.2 0.0 reduce-scatter.2.cloned.1.call-start
  7.9 1.2 dynamic-slice
  9.1 0.8 dynamic-update-slice
  9.9 13.8 %all-reduce = s32[16]{0:T(128)S(1)} all-reduce(s32[16]{0:T(128)S(1)} %dynamic-update-slice), channel_id=1, replica_groups=mesh['groups'=2,'dp'=16] {'dp'}, use_global_device_ids=true, to_apply=%add | all-reduce | flops 16 | bytes 128
  23.6 1.2 copy.22
  24.9 0.3 copy.23
  25.2 6.4 %copy.20 = bf16[256,8192]{0,1:T(8,128)(2,1)} copy(bf16[256,8192]{1,0:T(8,128)(2,1)} %param.5) | data formatting | bytes 8388608 | tf_op args[0]
  31.5 6.4 %copy.21 = bf16[256,64,128]{2,0,1:T(8,128)(2,1)} copy(bf16[256,64,128]{0,2,1:T(8,128)(2,1)} %bitcast.30) | data formatting | bytes 8388608 | tf_op jit(solution)/shard_map/reshape | solution.py:39
  37.9 0.7 gather_fusion.1
  38.7 2.9 %gather_fusion = bf16[16,256,128]{2,1,0:T(8,128)(2,1)S(1)} fusion(bf16[256,64,128]{2,0,1:T(8,128)(2,1)} %copy.21, s32[1024]{0:T(1024)S(1)} %get-tuple-element.17), kind=kCustom, calls=%fused_computation | custom fusion | bytes 2097216 | tf_op jit(solution)/shard_map/jit(_take)/gather | solution.py:41
  41.6 1.5 fusion.1
  43.2 0.0 reduce-scatter.2.cloned.1.call-update
  43.2 0.0 all-gather.2.cloned.1.call-start
  43.3 0.0 copy-done.2
  43.3 19.4 %all_gather.10 = bf16[16,128,128]{2,1,0:T(8,128)(2,1)S(1)} all-gather(bf16[1,128,128]{2,1,0:T(8,128)(2,1)S(1)} %copy-done.2), channel_id=1, replica_groups=mesh['groups'=2,'dp'=16] {'dp'}, dimensions={0}, use_global_device_ids=true | all-gather | bytes 557056 | tf_op jit(solution)/shard_map/all_gather | solution.py:21
  62.6 6.3 %broadcast_in_dim.27 = bf16[64,128,8,128]{3,1,2,0:T(8,128)(2,1)} broadcast(bf16[]{:T(256)} %constant.62.clone.1), dimensions={} | broadcast | bytes 16777218 | tf_op jit(solution)/shard_map/broadcast_in_dim | solution.py:15
  69.0 2.8 %scatter_fusion = bf16[64,128,8,128]{3,1,2,0:T(8,128)(2,1)} fusion(bf16[64,128,8,128]{3,1,2,0:T(8,128)(2,1)} %broadcast_in_dim.27, s32[16]{0:T(128)S(1)} %fusion.10, bf16[16,128,128]{2,1,0:T(8,128)(2,1)S(1)} %all_gather.10), kind=kCustom, calls=%fused_computation.2 | custom fusion | bytes 1572992 | tf_op jit(solution)/shard_map/scatter | solution.py:16
  71.7 16.8 %copy.19 = bf16[64,128,8,128]{3,2,1,0:T(8,128)(2,1)S(1)} copy(bf16[64,128,8,128]{3,1,2,0:T(8,128)(2,1)} %scatter_fusion) | data formatting | bytes 33554432 | tf_op jit(solution)/shard_map/scatter | solution.py:16
  88.6 0.0 copy-start
  88.6 0.0 copy-start.1
  88.6 9.1 %copy.29 = bf16[1024,8,8,128]{3,1,2,0:T(8,128)(2,1)} copy(bf16[1024,8,8,128]{3,2,1,0:T(8,128)(2,1)S(1)} %bitcast.28) | data formatting | bytes 33554432
  97.7 0.0 copy-done
  97.7 2.6 %add_convert_fusion = bf16[512,1024]{1,0:T(8,128)(2,1)} fusion(bf16[512,1024]{1,0:T(8,128)(2,1)S(1)} %copy-done, bf16[8192,1024]{1,0:T(8,128)(2,1)} %bitcast.29, s32[]{:T(128)S(6)} %select_n.40), kind=kLoop, calls=%fused_computation.6 | loop fusion | flops 2097152 | bytes 3145732 | tf_op jit(solution)/shard_map/convert_element_type | solution.py:31
  100.3 0.0 all-gather.2.cloned.1.call-update
  100.3 0.0 reduce-scatter.2.cloned.1.call-done
  100.4 1.5 broadcast_multiply_fusion
  101.8 124.9 %all-gather.2.cloned.1.call-done = bf16[8192,1024]{1,0:T(8,128)(2,1)} async-done(((bf16[512,1024]{1,0:T(8,128)(2,1)}), bf16[8192,1024]{1,0:T(8,128)(2,1)}) %all-gather.2.cloned.1.call-update) | async-done | bytes 16777232 | tf_op jit(solution)/shard_map/all_gather | solution.py:34
  226.7 0.0 copy-done.1
  226.7 12.3 %fusion = bf16[256,8192]{0,1:T(8,128)(2,1)} fusion(bf16[8192,1024]{1,0:T(8,128)(2,1)} %all-gather.2.cloned.1.call-done, bf16[256,1024]{1,0:T(8,128)(2,1)S(1)} %copy-done.1), kind=kOutput, calls=%fused_computation.5 | convolution fusion | flops 4297064448 | bytes 21495808 | tf_op jit(solution)/shard_map/dot_general | solution.py:32
  239.0 6.3 %copy.25 = bf16[256,8192]{1,0:T(8,128)(2,1)} copy(bf16[256,8192]{0,1:T(8,128)(2,1)} %fusion) | data formatting | bytes 8388608
  (4 shorter events, 0.0 us)
Async XLA Ops:
  7.2 36.1 %copy-start.2 = (bf16[1,128,128]{2,1,0:T(8,128)(2,1)S(1)}, bf16[1,128,128]{2,1,0:T(8,128)(2,1)}, u32[]{:S(2)}) copy-start(bf16[1,128,128]{2,1,0:T(8,128)(2,1)} %param.9) | copy-start | bytes 98308
  7.2 93.2 %reduce-scatter.2.cloned.1.call-start = ((), (), s32[]{:S(2)}) async-start(), calls=%async_computation.2 | async-start | bytes 1114112 | tf_op jit(solution)/shard_map/reduce_scatter | solution.py:43
  43.2 183.5 %all-gather.2.cloned.1.call-start = ((), (), s32[]{:S(2)}) async-start(), calls=%async_computation.1 | async-start | bytes 17825792 | tf_op jit(solution)/shard_map/all_gather | solution.py:34
  88.6 9.1 %copy-start = (bf16[512,1024]{1,0:T(8,128)(2,1)S(1)}, bf16[512,1024]{1,0:T(8,128)(2,1)}, u32[]{:S(2)}) copy-start(bf16[512,1024]{1,0:T(8,128)(2,1)} %param.7) | copy-start | bytes 3145732
  88.6 138.2 %copy-start.1 = (bf16[256,1024]{1,0:T(8,128)(2,1)S(1)}, bf16[256,1024]{1,0:T(8,128)(2,1)}, u32[]{:S(2)}) copy-start(bf16[256,1024]{1,0:T(8,128)(2,1)} %param.6) | copy-start | bytes 1572868
Sparse Core Ops, SparseCore 0:
  43.3 55.1 reduce-scatter.1
  101.3 125.3 all-gather.1
where the time goes:
time: 253 us; the launch traced here: 252 us
  waiting for transfers between devices  125 us (49%)
  local copies, waits for them, and re-layouts  61.3 us (24%)
  blocking collectives  33.1 us (13%)
  between operations  14.8 us (6%)
  matrix products  13.8 us (5%)
  other arithmetic  4.11 us (2%)
    all_gather x1, waiting for transfers between devices, body(): lax.all_gather(merged, 'dp', axis=0, tiled=True)  125 us
    unnamed x13, local copies, waits for them, and re-layouts  25.1 us
    scatter x2, local copies, waits for them, and re-layouts, delta_matrix(): field = field.at[tile_rows, :, tile_cols, :].set(tile_delta)  19.6 us
    all_gather x1, blocking collectives, whole_field(): all_deltas = lax.all_gather(tile_delta, 'dp', axis=0, tiled=True)  19.4 us
    unnamed x1, blocking collectives  13.8 us
    dot_general x1, matrix products, body(): lax.dot_general(grad_values, lax.all_gather(merged, 'dp', axis=0, tiled=T...  12.3 us
    reshape x1, local copies, waits for them, and re-layouts, body(): input_panels = layer_input.reshape(tokens_here, ROW_TILES, TILE)  6.37 us
    broadcast_in_dim x1, local copies, waits for them, and re-layouts, delta_matrix(): field = jnp.zeros((ROW_TILES, TILE, COL_TILES, TILE), tile_delta.dtype)  6.31 us
  transfers between devices with their start and end apart: 2, of which 1 were waited for; matrix products, arithmetic and copies ran while one was open for 16% of the time, Pallas kernels for 0%

commit v1 on v0

--- a/solution.py
+++ b/solution.py
@@ -7,6 +7,28 @@
 TILE = 128
 ROW_TILES = 64
 COL_TILES = 8
+
+
+def in_order(blocks, dim):
+    blocks = jnp.moveaxis(blocks, 0, dim)
+    lengths = blocks.shape
+    return blocks.reshape(*lengths[:dim], lengths[dim] * lengths[dim + 1], *lengths[dim + 2 :])
+
+
+def ring_gather(value, axis, dim):
+    peers = lax.axis_size(axis)
+    pairs = [(i, (i + 1) % peers) for i in range(peers)]
+    back = [(b, a) for a, b in pairs]
+    lower, upper = ([], [])
+    for step in range(peers - 1):
+        if step % 2 == 0:
+            lower.append(lax.ppermute(lower[-1] if lower else value, axis, pairs))
+        else:
+            upper.append(lax.ppermute(upper[-1] if upper else value, axis, back))
+    pieces = jnp.stack([*lower[::-1], value, *upper])
+    shift = lax.axis_index(axis) - len(lower)
+    pieces = pieces[(jnp.arange(peers) - shift) % peers]
+    return in_order(pieces, dim)
 
 
 def delta_matrix(tile_ids, tile_delta):
@@ -31,7 +53,7 @@
     merged = (base_weight.astype(jnp.float32) + own_field.astype(jnp.float32)).astype(jnp.bfloat16)
     grad_input = lax.dot_general(
         grad_values,
-        lax.all_gather(merged, "dp", axis=0, tiled=True),
+        ring_gather(merged, "dp", 0),
         (((1,), (1,)), ((), ())),
         preferred_element_type=jnp.float32,
     ).astype(jnp.bfloat16)

time: 253 us -> 357 us (1.41)
  starting transfers between devices: 0.08 us -> 115 us
  waiting for transfers between devices: 125 us -> 67.1 us
  local copies, waits for them, and re-layouts: 61.3 us -> 108 us
    all_gather x1 -> x0, waiting for transfers between devices: 125 us -> none  [body(): lax.all_gather(merged, 'dp', axis=0, tiled=True)]
    ppermute x0 -> x15, starting transfers between devices: none -> 115 us  [the longest x8 105 us: ring_gather(): lower.append(lax.ppermute(lower[-1] if lower else value, axis, pairs))]
    ppermute x0 -> x15, waiting for transfers between devices: none -> 35.9 us  [the longest x8 34.2 us: ring_gather(): lower.append(lax.ppermute(lower[-1] if lower else value, axis, pairs))]
    unnamed x13 -> x42, local copies, waits for them, and re-layouts: 25.1 us -> 56.6 us
    reduce_scatter x1, waiting for transfers between devices: 0.02 us -> 31.2 us  [body(): lax.psum_scatter(jnp.einsum('tja,tjb->jab', rows_taken, cols_taken, prefe...]
    gather x0 -> x1, local copies, waits for them, and re-layouts: none -> 13 us  [ring_gather(): pieces = pieces[(jnp.arange(peers) - shift) % peers]]
  transfers between devices with their start and end apart: 2 -> 16, of which waited for: 1 -> 8; matrix products, arithmetic and copies ran while one was open for 16% -> 15% of each run, Pallas kernels for 0% -> 0%
where the time goes in v1:
time: 357 us; the launch traced here: 356 us
  starting transfers between devices  115 us (32%)
  local copies, waits for them, and re-layouts  108 us (30%)
  waiting for transfers between devices  67.1 us (19%)
  blocking collectives  33.4 us (9%)
  matrix products  15.1 us (4%)
  between operations  14.8 us (4%)
    ppermute x8, starting transfers between devices, ring_gather(): lower.append(lax.ppermute(lower[-1] if lower else value, axis, pairs))  105 us
    unnamed x42, local copies, waits for them, and re-layouts  56.6 us
    ppermute x8, waiting for transfers between devices, ring_gather(): lower.append(lax.ppermute(lower[-1] if lower else value, axis, pairs))  34.2 us
    reduce_scatter x1, waiting for transfers between devices, body(): lax.psum_scatter(jnp.einsum('tja,tjb->jab', rows_taken, cols_taken, prefe...  31.2 us
    all_gather x1, blocking collectives, whole_field(): all_deltas = lax.all_gather(tile_delta, 'dp', axis=0, tiled=True)  19.6 us
    scatter x2, local copies, waits for them, and re-layouts, delta_matrix(): field = field.at[tile_rows, :, tile_cols, :].set(tile_delta)  19.6 us
    unnamed x1, blocking collectives  13.8 us
    gather x1, local copies, waits for them, and re-layouts, ring_gather(): pieces = pieces[(jnp.arange(peers) - shift) % peers]  13 us
  transfers between devices with their start and end apart: 16, of which 8 were waited for; matrix products, arithmetic and copies ran while one was open for 15% of the time, Pallas kernels for 0%

profile of v1, /device:TPU:0, one launch (start us, length us, event | category | flops | bytes accessed | tf_op | source)
XLA Modules:
  0.0 356.1 jit_solution(1918013126425023715)
XLA Ops:
  7.9 1.2 dynamic-slice
  9.9 13.8 %all-reduce = s32[16]{0:T(128)S(1)} all-reduce(s32[16]{0:T(128)S(1)} %dynamic-update-slice), channel_id=1, replica_groups=mesh['groups'=2,'dp'=16] {'dp'}, use_global_device_ids=true, to_apply=%add | all-reduce | flops 16 | bytes 128
  23.6 19.6 %all_gather.7 = bf16[16,128,128]{2,1,0:T(8,128)(2,1)S(1)} all-gather(bf16[1,128,128]{2,1,0:T(8,128)(2,1)} %param.9), channel_id=1, replica_groups=mesh['groups'=2,'dp'=16] {'dp'}, dimensions={0}, use_global_device_ids=true | all-gather | bytes 557056 | tf_op jit(solution)/shard_map/all_gather | solution.py:43
  43.3 6.3 %broadcast_in_dim.28 = bf16[64,128,8,128]{3,1,2,0:T(8,128)(2,1)} broadcast(bf16[]{:T(256)} %constant.73.clone.1), dimensions={} | broadcast | bytes 16777218 | tf_op jit(solution)/shard_map/broadcast_in_dim | solution.py:37
  49.6 2.8 scatter_fusion
  52.4 16.8 %copy.19 = bf16[64,128,8,128]{3,2,1,0:T(8,128)(2,1)S(1)} copy(bf16[64,128,8,128]{3,1,2,0:T(8,128)(2,1)} %scatter_fusion) | data formatting | bytes 33554432 | tf_op jit(solution)/shard_map/scatter | solution.py:38
  69.2 9.1 %copy.29 = bf16[1024,8,8,128]{3,1,2,0:T(8,128)(2,1)} copy(bf16[1024,8,8,128]{3,2,1,0:T(8,128)(2,1)S(1)} %bitcast.63) | data formatting | bytes 33554432
  78.4 1.7 add_convert_fusion
  80.5 16.6 %collective-permute-done = bf16[512,1024]{1,0:T(8,128)(2,1)S(1)} collective-permute-done((bf16[512,1024]{1,0:T(8,128)(2,1)S(1)}, bf16[512,1024]{1,0:T(8,128)(2,1)S(1)}, u32[]{:S(2)}, u32[]{:S(2)}) %collective-permute-start) | collective-permute-done | bytes 1048608 | tf_op jit(solution)/shard_map/ppermute | solution.py:25
  97.0 4.4 %collective-permute-start.8 = (bf16[512,1024]{1,0:T(8,128)(2,1)S(1)}, bf16[512,1024]{1,0:T(8,128)(2,1)S(1)}, u32[]{:S(2)}, u32[]{:S(2)}) collective-permute-start(bf16[512,1024]{1,0:T(8,128)(2,1)S(1)} %add_convert_fusion), channel_id=1, source_target_pairs={{1,0},{2,1},{3,2},{4,3},{5,4},{6,5},{7,6},{8,7},{9,8},{10,9},{11,1... | collective-permute-start | bytes 3145736 | tf_op jit(solution)/shard_map/ppermute | solution.py:27
  101.5 12.6 %collective-permute-done.1 = bf16[512,1024]{1,0:T(8,128)(2,1)S(1)} collective-permute-done((bf16[512,1024]{1,0:T(8,128)(2,1)S(1)}, bf16[512,1024]{1,0:T(8,128)(2,1)S(1)}, u32[]{:S(2)}, u32[]{:S(2)}) %collective-permute-start.1) | collective-permute-done | bytes 1048608 | tf_op jit(solution)/shard_map/ppermute | solution.py:25
  114.1 15.8 %collective-permute-start.2 = (bf16[512,1024]{1,0:T(8,128)(2,1)S(1)}, bf16[512,1024]{1,0:T(8,128)(2,1)S(1)}, u32[]{:S(2)}, u32[]{:S(2)}) collective-permute-start(bf16[512,1024]{1,0:T(8,128)(2,1)S(1)} %collective-permute-done.1), channel_id=1, source_target_pairs={{0,1},{1,2},{2,3},{3,4},{4,5},{5,6},{6,7},{7,8},{8,9},{9,10},{10,1... | collective-permute-start | bytes 3145736 | tf_op jit(solution)/shard_map/ppermute | solution.py:25
  130.8 1.3 collective-permute-done.2
  132.1 23.2 %collective-permute-start.3 = (bf16[512,1024]{1,0:T(8,128)(2,1)S(1)}, bf16[512,1024]{1,0:T(8,128)(2,1)S(1)}, u32[]{:S(2)}, u32[]{:S(2)}) collective-permute-start(bf16[512,1024]{1,0:T(8,128)(2,1)S(1)} %collective-permute-done.2), channel_id=1, source_target_pairs={{0,1},{1,2},{2,3},{3,4},{4,5},{5,6},{6,7},{7,8},{8,9},{9,10},{10,1... | collective-permute-start | bytes 3145736 | tf_op jit(solution)/shard_map/ppermute | solution.py:25
  156.3 1.3 collective-permute-done.3
  157.6 23.2 %collective-permute-start.4 = (bf16[512,1024]{1,0:T(8,128)(2,1)S(1)}, bf16[512,1024]{1,0:T(8,128)(2,1)}, u32[]{:S(2)}, u32[]{:S(2)}) collective-permute-start(bf16[512,1024]{1,0:T(8,128)(2,1)S(1)} %collective-permute-done.3), channel_id=1, source_target_pairs={{0,1},{1,2},{2,3},{3,4},{4,5},{5,6},{6,7},{7,8},{8,9},{9,10},{10,1... | collective-permute-start | bytes 3145736 | tf_op jit(solution)/shard_map/ppermute | solution.py:25
  180.8 2.4 collective-permute-done.4
  183.2 11.8 %collective-permute-start.5 = (bf16[512,1024]{1,0:T(8,128)(2,1)}, bf16[512,1024]{1,0:T(8,128)(2,1)}, u32[]{:S(2)}, u32[]{:S(2)}) collective-permute-start(bf16[512,1024]{1,0:T(8,128)(2,1)} %collective-permute-done.4), channel_id=1, source_target_pairs={{0,1},{1,2},{2,3},{3,4},{4,5},{5,6},{6,7},{7,8},{8,9},{9,10},{10,1... | collective-permute-start | bytes 3145736 | tf_op jit(solution)/shard_map/ppermute | solution.py:25
  195.0 6.4 %copy.20 = bf16[256,8192]{0,1:T(8,128)(2,1)} copy(bf16[256,8192]{1,0:T(8,128)(2,1)} %param.5) | data formatting | bytes 8388608 | tf_op args[0]
  201.3 6.4 %copy.21 = bf16[256,64,128]{2,0,1:T(8,128)(2,1)} copy(bf16[256,64,128]{0,2,1:T(8,128)(2,1)} %bitcast.66) | data formatting | bytes 8388608 | tf_op jit(solution)/shard_map/reshape | solution.py:61
  208.2 2.9 gather_fusion.1
  211.1 1.7 gather_fusion.2
  212.8 8.1 %collective-permute-start.6 = (bf16[512,1024]{1,0:T(8,128)(2,1)}, bf16[512,1024]{1,0:T(8,128)(2,1)}, u32[]{:S(2)}, u32[]{:S(2)}) collective-permute-start(bf16[512,1024]{1,0:T(8,128)(2,1)} %collective-permute-done.5), channel_id=1, source_target_pairs={{0,1},{1,2},{2,3},{3,4},{4,5},{5,6},{6,7},{7,8},{8,9},{9,10},{10,1... | collective-permute-start | bytes 3145736 | tf_op jit(solution)/shard_map/ppermute | solution.py:25
  220.8 2.8 fusion.1
  223.7 1.7 collective-permute-done.12
  225.4 4.7 %collective-permute-start.13 = (bf16[512,1024]{1,0:T(8,128)(2,1)}, bf16[512,1024]{1,0:T(8,128)(2,1)}, u32[]{:S(2)}, u32[]{:S(2)}) collective-permute-start(bf16[512,1024]{1,0:T(8,128)(2,1)} %collective-permute-done.12), channel_id=1, source_target_pairs={{1,0},{2,1},{3,2},{4,3},{5,4},{6,5},{7,6},{8,7},{9,8},{10,9},{11,1... | collective-permute-start | bytes 3145736 | tf_op jit(solution)/shard_map/ppermute | solution.py:27
  230.2 22.9 %collective-permute-start.7 = (bf16[512,1024]{1,0:T(8,128)(2,1)}, bf16[512,1024]{1,0:T(8,128)(2,1)}, u32[]{:S(2)}, u32[]{:S(2)}) collective-permute-start(bf16[512,1024]{1,0:T(8,128)(2,1)} %collective-permute-done.6), channel_id=1, source_target_pairs={{0,1},{1,2},{2,3},{3,4},{4,5},{5,6},{6,7},{7,8},{8,9},{9,10},{10,1... | collective-permute-start | bytes 3145736 | tf_op jit(solution)/shard_map/ppermute | solution.py:25
  253.1 31.2 %reduce-scatter.2.cloned.1.call-done = f32[1,128,128]{2,1,0:T(8,128)} async-done(((f32[16,128,128]{2,1,0:T(8,128)}), f32[1,128,128]{2,1,0:T(8,128)}) %reduce-scatter.2.cloned.1.call-update) | async-done | bytes 65552 | tf_op jit(solution)/shard_map/reduce_scatter | solution.py:65
  284.3 1.6 broadcast_multiply_fusion
  285.9 2.3 bitcast_dynamic-update-slice_fusion.15
  288.2 2.3 bitcast_dynamic-update-slice_fusion.14
  290.5 2.3 bitcast_dynamic-update-slice_fusion.13
  292.7 2.3 bitcast_dynamic-update-slice_fusion.12
  295.0 2.3 bitcast_dynamic-update-slice_fusion.11
  297.3 2.3 bitcast_dynamic-update-slice_fusion.10
  299.6 2.3 bitcast_dynamic-update-slice_fusion.9
  301.8 2.3 bitcast_dynamic-update-slice_fusion.8
  304.2 1.1 bitcast_dynamic-update-slice_fusion.7
  305.3 1.1 bitcast_dynamic-update-slice_fusion.6
  306.4 1.0 bitcast_dynamic-update-slice_fusion.5
  307.4 2.3 bitcast_dynamic-update-slice_fusion.4
  309.7 2.3 bitcast_dynamic-update-slice_fusion.3
  312.0 2.3 bitcast_dynamic-update-slice_fusion.2
  314.3 2.3 bitcast_dynamic-update-slice_fusion.1
  316.6 1.0 bitcast_dynamic-update-slice_fusion
  317.6 13.0 %gather_fusion = bf16[16,512,1024]{2,1,0:T(8,128)(2,1)} fusion(bf16[16,512,1024]{2,1,0:T(8,128)(2,1)} %bitcast_dynamic-update-slice_fusion, s32[1024]{0:T(1024)S(1)} %pad_clamp_fusion.2), kind=kCustom, calls=%fused_computation | custom fusion | bytes 33554496 | tf_op jit(solution)/shard_map/gather | solution.py:30
  330.7 12.3 %fusion = bf16[256,8192]{0,1:T(8,128)(2,1)} fusion(bf16[8192,1024]{1,0:T(8,128)(2,1)} %bitcast.65, bf16[256,1024]{1,0:T(8,128)(2,1)S(1)} %copy-done.9), kind=kOutput, calls=%fused_computation.6 | convolution fusion | flops 4297064448 | bytes 21495808 | tf_op jit(solution)/shard_map/dot_general | solution.py:54
  343.0 6.3 %copy.25 = bf16[256,8192]{1,0:T(8,128)(2,1)} copy(bf16[256,8192]{0,1:T(8,128)(2,1)} %fusion) | data formatting | bytes 8388608
  (47 shorter events, 3.9 us)
Async XLA Ops:
  7.2 277.1 %reduce-scatter.2.cloned.1.call-start = ((), (), s32[]{:S(2)}) async-start(), calls=%async_computation.1 | async-start | bytes 1114112 | tf_op jit(solution)/shard_map/reduce_scatter | solution.py:65
  69.2 9.1 %copy-start = (bf16[512,1024]{1,0:T(8,128)(2,1)S(1)}, bf16[512,1024]{1,0:T(8,128)(2,1)}, u32[]{:S(2)}) copy-start(bf16[512,1024]{1,0:T(8,128)(2,1)} %param.7) | copy-start | bytes 3145732
  78.4 129.3 %copy-start.9 = (bf16[256,1024]{1,0:T(8,128)(2,1)S(1)}, bf16[256,1024]{1,0:T(8,128)(2,1)}, u32[]{:S(2)}) copy-start(bf16[256,1024]{1,0:T(8,128)(2,1)} %param.6) | copy-start | bytes 1572868
  80.1 17.0 %collective-permute-start = (bf16[512,1024]{1,0:T(8,128)(2,1)S(1)}, bf16[512,1024]{1,0:T(8,128)(2,1)S(1)}, u32[]{:S(2)}, u32[]{:S(2)}) collective-permute-start(bf16[512,1024]{1,0:T(8,128)(2,1)S(1)} %add_convert_fusion), channel_id=1, source_target_pairs={{0,1},{1,2},{2,3},{3,4},{4,5},{5,6},{6,7},{7,8},{8,9},{9,10},{10,1... | collective-permute-start | bytes 3145736 | tf_op jit(solution)/shard_map/ppermute | solution.py:25
  97.0 32.8 %copy-start.1 = (bf16[512,1024]{1,0:T(8,128)(2,1)}, bf16[512,1024]{1,0:T(8,128)(2,1)S(1)}, u32[]{:S(2)}) copy-start(bf16[512,1024]{1,0:T(8,128)(2,1)S(1)} %collective-permute-done) | copy-start | bytes 3145732
  97.0 17.0 %collective-permute-start.1 = (bf16[512,1024]{1,0:T(8,128)(2,1)S(1)}, bf16[512,1024]{1,0:T(8,128)(2,1)S(1)}, u32[]{:S(2)}, u32[]{:S(2)}) collective-permute-start(bf16[512,1024]{1,0:T(8,128)(2,1)S(1)} %collective-permute-done), channel_id=1, source_target_pairs={{0,1},{1,2},{2,3},{3,4},{4,5},{5,6},{6,7},{7,8},{8,9},{9,10},{10,1... | collective-permute-start | bytes 3145736 | tf_op jit(solution)/shard_map/ppermute | solution.py:25
  97.0 32.8 %collective-permute-start.8 = (bf16[512,1024]{1,0:T(8,128)(2,1)S(1)}, bf16[512,1024]{1,0:T(8,128)(2,1)S(1)}, u32[]{:S(2)}, u32[]{:S(2)}) collective-permute-start(bf16[512,1024]{1,0:T(8,128)(2,1)S(1)} %add_convert_fusion), channel_id=1, source_target_pairs={{1,0},{2,1},{3,2},{4,3},{5,4},{6,5},{7,6},{8,7},{9,8},{10,9},{11,1... | collective-permute-start | bytes 3145736 | tf_op jit(solution)/shard_map/ppermute | solution.py:27
  114.1 41.2 %copy-start.4 = (bf16[512,1024]{1,0:T(8,128)(2,1)}, bf16[512,1024]{1,0:T(8,128)(2,1)S(1)}, u32[]{:S(2)}) copy-start(bf16[512,1024]{1,0:T(8,128)(2,1)S(1)} %collective-permute-done.1) | copy-start | bytes 3145732
  114.1 18.0 %collective-permute-start.2 = (bf16[512,1024]{1,0:T(8,128)(2,1)S(1)}, bf16[512,1024]{1,0:T(8,128)(2,1)S(1)}, u32[]{:S(2)}, u32[]{:S(2)}) collective-permute-start(bf16[512,1024]{1,0:T(8,128)(2,1)S(1)} %collective-permute-done.1), channel_id=1, source_target_pairs={{0,1},{1,2},{2,3},{3,4},{4,5},{5,6},{6,7},{7,8},{8,9},{9,10},{10,1... | collective-permute-start | bytes 3145736 | tf_op jit(solution)/shard_map/ppermute | solution.py:25
  129.8 1.0 copy-start.2
  129.8 25.5 %collective-permute-start.9 = (bf16[512,1024]{1,0:T(8,128)(2,1)S(1)}, bf16[512,1024]{1,0:T(8,128)(2,1)S(1)}, u32[]{:S(2)}, u32[]{:S(2)}) collective-permute-start(bf16[512,1024]{1,0:T(8,128)(2,1)S(1)} %collective-permute-done.8), channel_id=1, source_target_pairs={{1,0},{2,1},{3,2},{4,3},{5,4},{6,5},{7,6},{8,7},{9,8},{10,9},{11,1... | collective-permute-start | bytes 3145736 | tf_op jit(solution)/shard_map/ppermute | solution.py:27
  132.1 48.6 %copy-start.7 = (bf16[512,1024]{1,0:T(8,128)(2,1)}, bf16[512,1024]{1,0:T(8,128)(2,1)S(1)}, u32[]{:S(2)}) copy-start(bf16[512,1024]{1,0:T(8,128)(2,1)S(1)} %collective-permute-done.2) | copy-start | bytes 3145732
  132.1 25.5 %collective-permute-start.3 = (bf16[512,1024]{1,0:T(8,128)(2,1)S(1)}, bf16[512,1024]{1,0:T(8,128)(2,1)S(1)}, u32[]{:S(2)}, u32[]{:S(2)}) collective-permute-start(bf16[512,1024]{1,0:T(8,128)(2,1)S(1)} %collective-permute-done.2), channel_id=1, source_target_pairs={{0,1},{1,2},{2,3},{3,4},{4,5},{5,6},{6,7},{7,8},{8,9},{9,10},{10,1... | collective-permute-start | bytes 3145736 | tf_op jit(solution)/shard_map/ppermute | solution.py:25
  155.3 1.0 copy-start.5
  155.3 25.5 %collective-permute-start.10 = (bf16[512,1024]{1,0:T(8,128)(2,1)S(1)}, bf16[512,1024]{1,0:T(8,128)(2,1)}, u32[]{:S(2)}, u32[]{:S(2)}) collective-permute-start(bf16[512,1024]{1,0:T(8,128)(2,1)S(1)} %collective-permute-done.9), channel_id=1, source_target_pairs={{1,0},{2,1},{3,2},{4,3},{5,4},{6,5},{7,6},{8,7},{9,8},{10,9},{11,1... | collective-permute-start | bytes 3145736 | tf_op jit(solution)/shard_map/ppermute | solution.py:27
  157.6 23.2 %copy-start.8 = (bf16[512,1024]{1,0:T(8,128)(2,1)}, bf16[512,1024]{1,0:T(8,128)(2,1)S(1)}, u32[]{:S(2)}) copy-start(bf16[512,1024]{1,0:T(8,128)(2,1)S(1)} %collective-permute-done.3) | copy-start | bytes 3145732
  157.6 25.6 %collective-permute-start.4 = (bf16[512,1024]{1,0:T(8,128)(2,1)S(1)}, bf16[512,1024]{1,0:T(8,128)(2,1)}, u32[]{:S(2)}, u32[]{:S(2)}) collective-permute-start(bf16[512,1024]{1,0:T(8,128)(2,1)S(1)} %collective-permute-done.3), channel_id=1, source_target_pairs={{0,1},{1,2},{2,3},{3,4},{4,5},{5,6},{6,7},{7,8},{8,9},{9,10},{10,1... | collective-permute-start | bytes 3145736 | tf_op jit(solution)/shard_map/ppermute | solution.py:25
  180.7 32.0 %collective-permute-start.11 = (bf16[512,1024]{1,0:T(8,128)(2,1)}, bf16[512,1024]{1,0:T(8,128)(2,1)}, u32[]{:S(2)}, u32[]{:S(2)}) collective-permute-start(bf16[512,1024]{1,0:T(8,128)(2,1)} %collective-permute-done.10), channel_id=1, source_target_pairs={{1,0},{2,1},{3,2},{4,3},{5,4},{6,5},{7,6},{8,7},{9,8},{10,9},{11,1... | collective-permute-start | bytes 3145736 | tf_op jit(solution)/shard_map/ppermute | solution.py:27
  183.2 29.6 %collective-permute-start.5 = (bf16[512,1024]{1,0:T(8,128)(2,1)}, bf16[512,1024]{1,0:T(8,128)(2,1)}, u32[]{:S(2)}, u32[]{:S(2)}) collective-permute-start(bf16[512,1024]{1,0:T(8,128)(2,1)} %collective-permute-done.4), channel_id=1, source_target_pairs={{0,1},{1,2},{2,3},{3,4},{4,5},{5,6},{6,7},{7,8},{8,9},{9,10},{10,1... | collective-permute-start | bytes 3145736 | tf_op jit(solution)/shard_map/ppermute | solution.py:25
  212.8 12.6 %collective-permute-start.12 = (bf16[512,1024]{1,0:T(8,128)(2,1)}, bf16[512,1024]{1,0:T(8,128)(2,1)}, u32[]{:S(2)}, u32[]{:S(2)}) collective-permute-start(bf16[512,1024]{1,0:T(8,128)(2,1)} %collective-permute-done.11), channel_id=1, source_target_pairs={{1,0},{2,1},{3,2},{4,3},{5,4},{6,5},{7,6},{8,7},{9,8},{10,9},{11,1... | collective-permute-start | bytes 3145736 | tf_op jit(solution)/shard_map/ppermute | solution.py:27
  212.8 17.4 %collective-permute-start.6 = (bf16[512,1024]{1,0:T(8,128)(2,1)}, bf16[512,1024]{1,0:T(8,128)(2,1)}, u32[]{:S(2)}, u32[]{:S(2)}) collective-permute-start(bf16[512,1024]{1,0:T(8,128)(2,1)} %collective-permute-done.5), channel_id=1, source_target_pairs={{0,1},{1,2},{2,3},{3,4},{4,5},{5,6},{6,7},{7,8},{8,9},{9,10},{10,1... | collective-permute-start | bytes 3145736 | tf_op jit(solution)/shard_map/ppermute | solution.py:25
  223.6 81.7 %copy-start.3 = (bf16[512,1024]{1,0:T(8,128)(2,1)S(1)}, bf16[512,1024]{1,0:T(8,128)(2,1)}, u32[]{:S(2)}) copy-start(bf16[512,1024]{1,0:T(8,128)(2,1)} %copy-done.2) | copy-start | bytes 3145732
  225.4 60.4 %collective-permute-start.13 = (bf16[512,1024]{1,0:T(8,128)(2,1)}, bf16[512,1024]{1,0:T(8,128)(2,1)}, u32[]{:S(2)}, u32[]{:S(2)}) collective-permute-start(bf16[512,1024]{1,0:T(8,128)(2,1)} %collective-permute-done.12), channel_id=1, source_target_pairs={{1,0},{2,1},{3,2},{4,3},{5,4},{6,5},{7,6},{8,7},{9,8},{10,9},{11,1... | collective-permute-start | bytes 3145736 | tf_op jit(solution)/shard_map/ppermute | solution.py:27
  230.2 55.7 %collective-permute-start.7 = (bf16[512,1024]{1,0:T(8,128)(2,1)}, bf16[512,1024]{1,0:T(8,128)(2,1)}, u32[]{:S(2)}, u32[]{:S(2)}) collective-permute-start(bf16[512,1024]{1,0:T(8,128)(2,1)} %collective-permute-done.6), channel_id=1, source_target_pairs={{0,1},{1,2},{2,3},{3,4},{4,5},{5,6},{6,7},{7,8},{8,9},{9,10},{10,1... | collective-permute-start | bytes 3145736 | tf_op jit(solution)/shard_map/ppermute | solution.py:25
  284.3 22.1 %copy-start.6 = (bf16[512,1024]{1,0:T(8,128)(2,1)S(1)}, bf16[512,1024]{1,0:T(8,128)(2,1)}, u32[]{:S(2)}) copy-start(bf16[512,1024]{1,0:T(8,128)(2,1)} %copy-done.5) | copy-start | bytes 3145732
  285.8 30.8 %collective-permute-start.14 = (bf16[512,1024]{1,0:T(8,128)(2,1)}, bf16[512,1024]{1,0:T(8,128)(2,1)S(1)}, u32[]{:S(2)}, u32[]{:S(2)}) collective-permute-start(bf16[512,1024]{1,0:T(8,128)(2,1)} %collective-permute-done.13), channel_id=1, source_target_pairs={{1,0},{2,1},{3,2},{4,3},{5,4},{6,5},{7,6},{8,7},{9,8},{10,9},{11,1... | collective-permute-start | bytes 3145736 | tf_op jit(solution)/shard_map/ppermute | solution.py:27
Sparse Core Ops, SparseCore 0:
  223.8 60.4 reduce-scatter.1
